TPU v7x, 32 devices: a whole 2x2x4 slice. The times are simulated.
32 devices in a mesh: shift: 4 (over y, x), rows: 8 (over z, core).
Axes of the slice: x: 2, y: 2, z: 4, core: 2. Of those that a mesh axis runs over, the one named last changes fastest.
Arguments:
- filtered: bfloat16 [4, 131072, 256], P('shift', 'rows'), as said below
- weights: float32 [4, 256], P('shift'), may hold values from 0.25 to 2
Outputs:
- basis: float32 [131072, 256], P(('rows', 'shift'))
- r_factor: float32 [256, 256], replicated
Inputs may be any that keep to these rules, and one draw needn't show every extreme that they name: Each filtered block is of full rank.
All inputs are finite; a program needn't handle non-finite values.
Results may differ from a plain program's by a relative error of at most 0.0003.
Values sent between devices are 32-bit elements; how exact they have to be, the bound alone decides.
No kernel may reach another device: no remote copies, remote signals or barrier semaphores. Data moves between devices by JAX's collectives and lax.ppermute only.
A program may use at most 128 MiB of HBM per device.

v0:
```python
import jax
import jax.numpy as jnp
from jax import lax
from jax.sharding import PartitionSpec as P


def cross_products(left, right):
    return jnp.dot(
        left.T, right, precision=lax.Precision.HIGHEST, preferred_element_type=jnp.float32
    )


def shards(filtered, weights):
    weighted = filtered[0].astype(jnp.float32) * weights[0][None, :]
    mixed = lax.psum_scatter(weighted, "shift", scatter_dimension=0, tiled=True)
    devices_all = lax.axis_size(("shift", "rows"))
    total_rows = mixed.shape[0] * devices_all
    gram = cross_products(mixed, mixed) / total_rows
    lower = jnp.linalg.cholesky(lax.psum(gram, ("shift", "rows")))
    basis = jax.scipy.linalg.solve_triangular(lower, mixed.T, lower=True).T
    return (basis, lower.T)


def solution(mesh):
    in_specs = (P("shift", "rows", None), P("shift", None))
    out_specs = (P(("rows", "shift"), None), P())
    return jax.shard_map(shards, mesh=mesh, in_specs=in_specs, out_specs=out_specs, check_vma=False)
```

profile of v0, /device:TPU:0, one launch (start us, length us, event | category | flops | bytes accessed | tf_op | source)
XLA Modules:
  0.0 396.4 jit_solution(7916319687444031821)
XLA Ops:
  7.2 0.0 reduce-scatter.2.cloned.1.call-start
  7.2 9.6 %convert_multiply_fusion = f32[16384,256]{1,0:T(8,128)} fusion(bf16[1,16384,256]{2,1,0:T(8,128)(2,1)} %param.2, f32[256]{0:T(256)} %bitcast.44), kind=kLoop, calls=%fused_computation.2 | loop fusion | flops 8388608 | bytes 25166848 | tf_op jit(solution)/shard_map/mul | solution.py:14
  16.8 0.0 reduce-scatter.2.cloned.1.call-update
  16.8 0.0 all-reduce.3.cloned.1.call-start
  16.9 156.7 %reduce-scatter.2.cloned.1.call-done = f32[4096,256]{1,0:T(8,128)} async-done(((f32[16384,256]{1,0:T(8,128)}), f32[4096,256]{1,0:T(8,128)}) %reduce-scatter.2.cloned.1.call-update) | async-done | bytes 4194320 | tf_op jit(solution)/shard_map/reduce_scatter | solution.py:15
  173.5 10.9 %convolution_multiply_fusion = f32[256,256]{0,1:T(8,128)} fusion(f32[4096,256]{1,0:T(8,128)} %reduce-scatter.2.cloned.1.call-done), kind=kOutput, calls=%fused_computation.7 | convolution fusion | flops 3221291008 | bytes 4456448 | tf_op jit(solution)/shard_map/dot_general | solution.py:8
  184.4 0.0 all-reduce.3.cloned.1.call-update
  184.5 125.1 %all-reduce.3.cloned.1.call-done = f32[256,256]{0,1:T(8,128)} async-done(((f32[256,256]{0,1:T(8,128)}), f32[256,256]{0,1:T(8,128)}) %all-reduce.3.cloned.1.call-update) | async-done | bytes 262160 | tf_op jit(solution)/shard_map/psum | solution.py:19
  309.6 1.1 copy.5
  310.7 1.0 fusion.2
  311.7 11.7 %cholesky.50 = f32[128,128]{1,0:T(8,128)S(1)} custom-call(f32[128,128]{1,0:T(8,128)S(1)} %cholesky.118), custom_call_target="Cholesky" | custom-call | tf_op jit(solution)/shard_map/jit(cholesky)/cholesky | solution.py:19
  323.4 10.0 %custom-call.15 = f32[1,128,128]{1,2,0:T(8,128)S(1)} custom-call(f32[1,128,128]{2,1,0:T(8,128)S(1)} %get-tuple-element.27), custom_call_target="InvertDiagBlocksLowerTriangular" | custom-call | tf_op jit(solution)/shard_map/jit(cholesky)/cholesky | solution.py:19
  333.4 0.2 constant_dynamic-update-slice_fusion.1
  333.7 0.3 convolution_subtract_fusion.1
  333.9 11.7 %cholesky.105 = f32[128,128]{1,0:T(8,128)S(1)} custom-call(f32[128,128]{1,0:T(8,128)S(1)} %convolution_subtract_fusion.1), custom_call_target="Cholesky" | custom-call | tf_op jit(solution)/shard_map/jit(cholesky)/cholesky | solution.py:19
  345.7 0.7 compare_reduce_fusion
  347.8 0.1 triangular_solve.57
  347.9 4.1 %while.1 = (s32[]{:T(128)}, f32[256,256]{1,0:T(8,128)S(1)}, s32[2,2]{1,0:T(2,128)S(1)}, f32[2,128,128]{2,1,0:T(8,128)S(1)}, s32[]{:T(128)}) while((s32[]{:T(128)}, f32[256,256]{1,0:T(8,128)S(1)}, s32[2,2]{1,0:T(2,128)S(1)}, f32[2,128,128]{2,1,0:T(8,128)S(1)}, s32[]{:T(128)}) %tuple.29), condition=%wide.while_cond, body=%wide.while_body.sunk | while | flops 2 | bytes 131181 | solution.py:20
  347.9 0.6 fusion.18
  348.5 1.4 bitcast_dynamic-update-slice_fusion.2
  349.9 0.6 fusion.18
  350.5 1.4 bitcast_dynamic-update-slice_fusion.2
  352.0 19.7 %custom-call.16 = f32[2,128,128]{1,2,0:T(8,128)S(1)} custom-call(f32[2,128,128]{2,1,0:T(8,128)S(1)} %get-tuple-element.9), custom_call_target="InvertDiagBlocksLowerTriangular" | custom-call | tf_op jit(solution)/shard_map/jit(_solve_triangular)/triangular_solve | solution.py:20
  371.6 0.0 copy-start
  371.6 3.7 fusion
  375.3 0.0 copy-done
  375.3 3.4 convolution_subtract_fusion
  378.8 2.0 fusion.6
  380.8 2.4 maximum_bitcast_fusion
  383.2 5.6 %copy.6 = f32[4096,256]{1,0:T(8,128)} copy(f32[4096,256]{0,1:T(8,128)} %maximum_bitcast_fusion) | data formatting | bytes 8388608
  388.8 0.8 copy.7
  (9 shorter events, 0.2 us)
Async XLA Ops:
  7.2 166.4 %reduce-scatter.2.cloned.1.call-start = ((), (), s32[]{:S(2)}) async-start(), calls=%async_computation.1 | async-start | bytes 20971520 | tf_op jit(solution)/shard_map/reduce_scatter | solution.py:15
  16.8 292.8 %all-reduce.3.cloned.1.call-start = ((), (), s32[]{:S(2)}) async-start(), calls=%async_computation.2 | async-start | bytes 524288 | tf_op jit(solution)/shard_map/psum | solution.py:19
  371.6 3.7 copy-start
Sparse Core Ops, SparseCore 0:
  17.0 156.5 reduce-scatter.1
  184.6 124.9 all-reduce.2
where the time goes:
time: 397 us; the launch traced here: 396 us
  waiting for transfers between devices  282 us (71%)
  other arithmetic  66.9 us (17%)
  matrix products  20.5 us (5%)
  between operations  15.5 us (4%)
  local copies, waits for them, and re-layouts  11.7 us (3%)
    reduce_scatter x1, waiting for transfers between devices, shards(): mixed = lax.psum_scatter(weighted, 'shift', scatter_dimension=0, tiled=True)  157 us
    psum x1, waiting for transfers between devices, shards(): lower = jnp.linalg.cholesky(lax.psum(gram, ('shift', 'rows')))  125 us
    another operation x6, other arithmetic, shards(): lower = jnp.linalg.cholesky(lax.psum(gram, ('shift', 'rows')))  34.2 us
    another operation x2, other arithmetic, shards(): basis = jax.scipy.linalg.solve_triangular(lower, mixed.T, lower=True).T  19.7 us
    dot_general x1, matrix products, cross_products(): jnp.dot(left.T, right, precision=lax.Precision.HIGHEST, preferred_element...  10.9 us
    mul x1, other arithmetic, shards(): weighted = filtered[0].astype(jnp.float32) * weights[0][None, :]  9.6 us
    another operation x3, matrix products, shards(): basis = jax.scipy.linalg.solve_triangular(lower, mixed.T, lower=True).T  9.09 us
  transfers between devices with their start and end apart: 2, of which 2 were waited for; matrix products, arithmetic and copies ran while one was open for 0% of the time, Pallas kernels for 0%

commit v1 on v0

--- a/solution.py
+++ b/solution.py
@@ -16,7 +16,8 @@
     devices_all = lax.axis_size(("shift", "rows"))
     total_rows = mixed.shape[0] * devices_all
     gram = cross_products(mixed, mixed) / total_rows
-    lower = jnp.linalg.cholesky(lax.psum(gram, ("shift", "rows")))
+    set_plate = lambda own_rows: lax.psum(lax.psum(own_rows, "rows"), "shift")
+    lower = jnp.linalg.cholesky(set_plate(gram))
     basis = jax.scipy.linalg.solve_triangular(lower, mixed.T, lower=True).T
     return (basis, lower.T)
 

time: 397 us -> 372 us (0.937)
  waiting for transfers between devices: 282 us -> 257 us
    psum x1 -> x2, waiting for transfers between devices: 125 us -> 99.9 us  [shards(): set_plate = lambda own_rows: lax.psum(lax.psum(own_rows, 'rows'), 'shift')]
  transfers between devices with their start and end apart: 2 -> 3, of which waited for: 2 -> 3; matrix products, arithmetic and copies ran while one was open for 0% -> 0% of each run, Pallas kernels for 0% -> 0%
where the time goes in v1:
time: 372 us; the launch traced here: 371 us
  waiting for transfers between devices  257 us (69%)
  other arithmetic  66.7 us (18%)
  matrix products  20.5 us (6%)
  between operations  15.2 us (4%)
  local copies, waits for them, and re-layouts  11.7 us (3%)
    reduce_scatter x1, waiting for transfers between devices, shards(): mixed = lax.psum_scatter(weighted, 'shift', scatter_dimension=0, tiled=True)  157 us
    psum x2, waiting for transfers between devices, shards(): set_plate = lambda own_rows: lax.psum(lax.psum(own_rows, 'rows'), 'shift')  99.9 us
    another operation x6, other arithmetic, shards(): lower = jnp.linalg.cholesky(set_plate(gram))  34 us
    another operation x2, other arithmetic, shards(): basis = jax.scipy.linalg.solve_triangular(lower, mixed.T, lower=True).T  19.7 us
    dot_general x1, matrix products, cross_products(): jnp.dot(left.T, right, precision=lax.Precision.HIGHEST, preferred_element...  10.9 us
    mul x1, other arithmetic, shards(): weighted = filtered[0].astype(jnp.float32) * weights[0][None, :]  9.6 us
    another operation x3, matrix products, shards(): basis = jax.scipy.linalg.solve_triangular(lower, mixed.T, lower=True).T  9.09 us
  transfers between devices with their start and end apart: 3, of which 3 were waited for; matrix products, arithmetic and copies ran while one was open for 0% of the time, Pallas kernels for 0%

profile of v1, /device:TPU:0, one launch (start us, length us, event | category | flops | bytes accessed | tf_op | source)
XLA Modules:
  0.0 371.2 jit_solution(14428343768684158041)
XLA Ops:
  7.2 0.0 reduce-scatter.2.cloned.1.call-start
  7.2 9.6 %convert_multiply_fusion = f32[16384,256]{1,0:T(8,128)} fusion(bf16[1,16384,256]{2,1,0:T(8,128)(2,1)} %param.2, f32[256]{0:T(256)} %bitcast.44), kind=kLoop, calls=%fused_computation.2 | loop fusion | flops 8388608 | bytes 25166848 | tf_op jit(solution)/shard_map/mul | solution.py:14
  16.8 0.0 reduce-scatter.2.cloned.1.call-update
  16.8 0.0 all-reduce.4.cloned.1.call-start
  16.9 156.7 %reduce-scatter.2.cloned.1.call-done = f32[4096,256]{1,0:T(8,128)} async-done(((f32[16384,256]{1,0:T(8,128)}), f32[4096,256]{1,0:T(8,128)}) %reduce-scatter.2.cloned.1.call-update) | async-done | bytes 4194320 | tf_op jit(solution)/shard_map/reduce_scatter | solution.py:15
  173.5 10.9 %convolution_multiply_fusion = f32[256,256]{0,1:T(8,128)} fusion(f32[4096,256]{1,0:T(8,128)} %reduce-scatter.2.cloned.1.call-done), kind=kOutput, calls=%fused_computation.7 | convolution fusion | flops 3221291008 | bytes 4456448 | tf_op jit(solution)/shard_map/dot_general | solution.py:8
  184.4 0.0 all-reduce.4.cloned.1.call-update
  184.5 0.2 all-reduce.6.cloned.1.call-start
  184.7 54.8 %all-reduce.4.cloned.1.call-done = f32[256,256]{0,1:T(8,128)} async-done(((f32[256,256]{0,1:T(8,128)}), f32[256,256]{0,1:T(8,128)}) %all-reduce.4.cloned.1.call-update) | async-done | bytes 262160 | tf_op jit(solution)/shard_map/psum | solution.py:19
  239.5 0.0 all-reduce.6.cloned.1.call-update
  239.6 45.1 %all-reduce.6.cloned.1.call-done = f32[256,256]{0,1:T(8,128)} async-done(((f32[256,256]{0,1:T(8,128)}), f32[256,256]{0,1:T(8,128)}) %all-reduce.6.cloned.1.call-update) | async-done | bytes 262160 | tf_op jit(solution)/shard_map/psum | solution.py:19
  284.6 1.1 copy.5
  285.7 1.0 fusion.2
  286.7 11.7 %cholesky.50 = f32[128,128]{1,0:T(8,128)S(1)} custom-call(f32[128,128]{1,0:T(8,128)S(1)} %cholesky.118), custom_call_target="Cholesky" | custom-call | tf_op jit(solution)/shard_map/jit(cholesky)/cholesky | solution.py:20
  298.5 9.8 %custom-call.15 = f32[1,128,128]{1,2,0:T(8,128)S(1)} custom-call(f32[1,128,128]{2,1,0:T(8,128)S(1)} %get-tuple-element.27), custom_call_target="InvertDiagBlocksLowerTriangular" | custom-call | tf_op jit(solution)/shard_map/jit(cholesky)/cholesky | solution.py:20
  308.3 0.2 constant_dynamic-update-slice_fusion.1
  308.5 0.3 convolution_subtract_fusion.1
  308.8 11.7 %cholesky.105 = f32[128,128]{1,0:T(8,128)S(1)} custom-call(f32[128,128]{1,0:T(8,128)S(1)} %convolution_subtract_fusion.1), custom_call_target="Cholesky" | custom-call | tf_op jit(solution)/shard_map/jit(cholesky)/cholesky | solution.py:20
  320.5 0.7 compare_reduce_fusion
  322.7 0.1 triangular_solve.57
  322.7 4.3 %while.1 = (s32[]{:T(128)}, f32[256,256]{1,0:T(8,128)S(1)}, s32[2,2]{1,0:T(2,128)S(1)}, f32[2,128,128]{2,1,0:T(8,128)S(1)}, s32[]{:T(128)}) while((s32[]{:T(128)}, f32[256,256]{1,0:T(8,128)S(1)}, s32[2,2]{1,0:T(2,128)S(1)}, f32[2,128,128]{2,1,0:T(8,128)S(1)}, s32[]{:T(128)}) %tuple.29), condition=%wide.while_cond, body=%wide.while_body.sunk | while | flops 2 | bytes 131181 | solution.py:21
  322.9 0.6 fusion.18
  323.5 1.4 bitcast_dynamic-update-slice_fusion.2
  325.0 0.6 fusion.18
  325.6 1.4 bitcast_dynamic-update-slice_fusion.2
  327.0 19.7 %custom-call.16 = f32[2,128,128]{1,2,0:T(8,128)S(1)} custom-call(f32[2,128,128]{2,1,0:T(8,128)S(1)} %get-tuple-element.9), custom_call_target="InvertDiagBlocksLowerTriangular" | custom-call | tf_op jit(solution)/shard_map/jit(_solve_triangular)/triangular_solve | solution.py:21
  346.7 0.0 copy-start
  346.7 3.7 fusion
  350.4 0.0 copy-done
  350.4 3.4 convolution_subtract_fusion
  353.8 2.0 fusion.6
  355.8 2.4 maximum_bitcast_fusion
  358.2 5.6 %copy.6 = f32[4096,256]{1,0:T(8,128)} copy(f32[4096,256]{0,1:T(8,128)} %maximum_bitcast_fusion) | data formatting | bytes 8388608
  363.8 0.8 copy.7
  (9 shorter events, 0.2 us)
Async XLA Ops:
  7.2 166.4 %reduce-scatter.2.cloned.1.call-start = ((), (), s32[]{:S(2)}) async-start(), calls=%async_computation.1 | async-start | bytes 20971520 | tf_op jit(solution)/shard_map/reduce_scatter | solution.py:15
  16.8 222.7 %all-reduce.4.cloned.1.call-start = ((), (), s32[]{:S(2)}) async-start(), calls=%async_computation.2 | async-start | bytes 524288 | tf_op jit(solution)/shard_map/psum | solution.py:19
  184.5 100.2 %all-reduce.6.cloned.1.call-start = ((), (), s32[]{:S(2)}) async-start(), calls=%async_computation.3 | async-start | bytes 524288 | tf_op jit(solution)/shard_map/psum | solution.py:19
  346.7 3.7 copy-start
Sparse Core Ops, SparseCore 0:
  17.0 156.5 reduce-scatter.1
  184.6 54.8 all-reduce.3
  242.7 41.8 all-reduce.5

commit v2 on v0

--- a/solution.py
+++ b/solution.py
@@ -2,6 +2,10 @@
 import jax.numpy as jnp
 from jax import lax
 from jax.sharding import PartitionSpec as P
+
+
+def slices_try_all(sample):
+    return jnp.sum(lax.all_gather(sample, ("shift", "rows")), axis=0)
 
 
 def cross_products(left, right):
@@ -16,7 +20,7 @@
     devices_all = lax.axis_size(("shift", "rows"))
     total_rows = mixed.shape[0] * devices_all
     gram = cross_products(mixed, mixed) / total_rows
-    lower = jnp.linalg.cholesky(lax.psum(gram, ("shift", "rows")))
+    lower = jnp.linalg.cholesky(slices_try_all(gram))
     basis = jax.scipy.linalg.solve_triangular(lower, mixed.T, lower=True).T
     return (basis, lower.T)
 

time: 397 us -> 351 us (0.88)
  waiting for transfers between devices: 282 us -> 234 us
    psum x1 -> x0, waiting for transfers between devices: 125 us -> none  [shards(): lower = jnp.linalg.cholesky(lax.psum(gram, ('shift', 'rows')))]
    all_gather x0 -> x1, waiting for transfers between devices: none -> 77.5 us  [slices_try_all(): return jnp.sum(lax.all_gather(sample, ('shift', 'rows')), axis=0)]
where the time goes in v2:
time: 351 us
  waiting for transfers between devices  234 us (67%)
  other arithmetic  69.8 us (20%)
  matrix products  20.5 us (6%)
  between operations  15.5 us (4%)
  local copies, waits for them, and re-layouts  10.7 us (3%)
    reduce_scatter x1, waiting for transfers between devices, shards(): mixed = lax.psum_scatter(weighted, 'shift', scatter_dimension=0, tiled=True)  157 us
    all_gather x1, waiting for transfers between devices, slices_try_all(): return jnp.sum(lax.all_gather(sample, ('shift', 'rows')), axis=0)  77.5 us
    another operation x6, other arithmetic, shards(): lower = jnp.linalg.cholesky(slices_try_all(gram))  34.2 us
    another operation x2, other arithmetic, shards(): basis = jax.scipy.linalg.solve_triangular(lower, mixed.T, lower=True).T  19.7 us
    dot_general x1, matrix products, cross_products(): jnp.dot(left.T, right, precision=lax.Precision.HIGHEST, preferred_element...  10.9 us
    mul x1, other arithmetic, shards(): weighted = filtered[0].astype(jnp.float32) * weights[0][None, :]  9.6 us
    another operation x3, matrix products, shards(): basis = jax.scipy.linalg.solve_triangular(lower, mixed.T, lower=True).T  9.09 us
  transfers between devices with their start and end apart: 2, of which 2 were waited for; matrix products, arithmetic and copies ran while one was open for 0% of the time, Pallas kernels for 0%

profile of v2, /device:TPU:0, one launch (start us, length us, event | category | flops | bytes accessed | tf_op | source)
XLA Modules:
  0.0 350.9 jit_solution(9389313986666459823)
XLA Ops:
  7.2 0.0 reduce-scatter.2.cloned.1.call-start
  7.2 9.6 %convert_multiply_fusion = f32[16384,256]{1,0:T(8,128)} fusion(bf16[1,16384,256]{2,1,0:T(8,128)(2,1)} %param.2, f32[256]{0:T(256)} %bitcast.46), kind=kLoop, calls=%fused_computation.2 | loop fusion | flops 8388608 | bytes 25166848 | tf_op jit(solution)/shard_map/mul | solution.py:18
  16.8 0.0 reduce-scatter.2.cloned.1.call-update
  16.8 0.0 all-gather.3.cloned.1.call-start
  16.9 156.7 %reduce-scatter.2.cloned.1.call-done = f32[4096,256]{1,0:T(8,128)} async-done(((f32[16384,256]{1,0:T(8,128)}), f32[4096,256]{1,0:T(8,128)}) %reduce-scatter.2.cloned.1.call-update) | async-done | bytes 4194320 | tf_op jit(solution)/shard_map/reduce_scatter | solution.py:19
  173.5 10.9 %convolution_multiply_fusion = f32[256,256]{1,0:T(8,128)} fusion(f32[4096,256]{1,0:T(8,128)} %reduce-scatter.2.cloned.1.call-done), kind=kOutput, calls=%fused_computation.7 | convolution fusion | flops 3221291008 | bytes 4456448 | tf_op jit(solution)/shard_map/dot_general | solution.py:12
  184.5 0.0 all-gather.3.cloned.1.call-update
  184.5 77.5 %all-gather.3.cloned.1.call-done = f32[8192,256]{1,0:T(8,128)} async-done(((f32[256,256]{1,0:T(8,128)}), f32[8192,256]{1,0:T(8,128)}) %all-gather.3.cloned.1.call-update) | async-done | bytes 8388624 | tf_op jit(solution)/shard_map/all_gather | solution.py:8
  262.0 3.9 %reduce_sum.9 = f32[256,256]{1,0:T(8,128)S(1)} reduce(f32[32,256,256]{2,1,0:T(8,128)} %bitcast.45, f32[]{:T(128)} %constant.78.clone.1), dimensions={0}, to_apply=%region_1.0 | reduce | flops 2031616 | bytes 8650756 | tf_op jit(solution)/shard_map/reduce_sum | solution.py:8
  266.0 0.1 copy.7
  266.1 11.7 %cholesky.50 = f32[128,128]{1,0:T(8,128)S(1)} custom-call(f32[128,128]{1,0:T(8,128)S(1)} %cholesky.118), custom_call_target="Cholesky" | custom-call | tf_op jit(solution)/shard_map/jit(cholesky)/cholesky | solution.py:23
  277.9 9.9 %custom-call.15 = f32[1,128,128]{1,2,0:T(8,128)S(1)} custom-call(f32[1,128,128]{2,1,0:T(8,128)S(1)} %get-tuple-element.29), custom_call_target="InvertDiagBlocksLowerTriangular" | custom-call | tf_op jit(solution)/shard_map/jit(cholesky)/cholesky | solution.py:23
  287.9 0.2 constant_dynamic-update-slice_fusion.1
  288.1 0.3 convolution_subtract_fusion.1
  288.3 11.7 %cholesky.105 = f32[128,128]{1,0:T(8,128)S(1)} custom-call(f32[128,128]{1,0:T(8,128)S(1)} %convolution_subtract_fusion.1), custom_call_target="Cholesky" | custom-call | tf_op jit(solution)/shard_map/jit(cholesky)/cholesky | solution.py:23
  300.1 0.7 compare_reduce_fusion
  302.2 0.1 triangular_solve.57
  302.3 4.1 %while.1 = (s32[]{:T(128)}, f32[256,256]{1,0:T(8,128)S(1)}, s32[2,2]{1,0:T(2,128)S(1)}, f32[2,128,128]{2,1,0:T(8,128)S(1)}, s32[]{:T(128)}) while((s32[]{:T(128)}, f32[256,256]{1,0:T(8,128)S(1)}, s32[2,2]{1,0:T(2,128)S(1)}, f32[2,128,128]{2,1,0:T(8,128)S(1)}, s32[]{:T(128)}) %tuple.30), condition=%wide.while_cond, body=%wide.while_body.sunk | while | flops 2 | bytes 131181 | solution.py:24
  302.3 0.6 fusion.18
  302.9 1.4 bitcast_dynamic-update-slice_fusion.2
  304.3 0.6 fusion.18
  304.9 1.4 bitcast_dynamic-update-slice_fusion.2
  306.4 19.7 %custom-call.16 = f32[2,128,128]{1,2,0:T(8,128)S(1)} custom-call(f32[2,128,128]{2,1,0:T(8,128)S(1)} %get-tuple-element.9), custom_call_target="InvertDiagBlocksLowerTriangular" | custom-call | tf_op jit(solution)/shard_map/jit(_solve_triangular)/triangular_solve | solution.py:24
  326.1 0.0 copy-start
  326.1 3.7 %fusion = f32[128,4096]{1,0:T(8,128)S(1)} fusion(f32[256,4096]{0,1:T(8,128)} %bitcast.43, f32[2,128,128]{1,2,0:T(8,128)S(1)} %custom-call.16), kind=kOutput, calls=%fused_computation.5 | convolution fusion | flops 805306368 | bytes 4259840 | tf_op jit(solution)/shard_map/jit(_solve_triangular)/triangular_solve | solution.py:24
  329.8 0.0 copy-done
  329.8 3.4 convolution_subtract_fusion
  333.2 2.0 fusion.6
  335.2 2.4 maximum_bitcast_fusion
  337.6 5.6 %copy.8 = f32[4096,256]{1,0:T(8,128)} copy(f32[4096,256]{0,1:T(8,128)} %maximum_bitcast_fusion) | data formatting | bytes 8388608
  343.2 0.8 copy.9
  (10 shorter events, 0.2 us)
Async XLA Ops:
  7.2 166.4 %reduce-scatter.2.cloned.1.call-start = ((), (), s32[]{:S(2)}) async-start(), calls=%async_computation.1 | async-start | bytes 20971520 | tf_op jit(solution)/shard_map/reduce_scatter | solution.py:19
  16.8 245.2 %all-gather.3.cloned.1.call-start = ((), (), s32[]{:S(2)}) async-start(), calls=%async_computation.2 | async-start | bytes 8650752 | tf_op jit(solution)/shard_map/all_gather | solution.py:8
  326.1 3.7 %copy-start = (f32[4096,256]{1,0:T(8,128)S(1)}, f32[4096,256]{1,0:T(8,128)}, u32[]{:S(2)}) copy-start(f32[4096,256]{1,0:T(8,128)} %reduce-scatter.2.cloned.1.call-done) | copy-start | bytes 12582916
Sparse Core Ops, SparseCore 0:
  17.0 156.5 reduce-scatter.1
  184.6 77.3 all-gather.2
